TPU v7x, 256 devices: a whole 4x4x8 slice. The times are simulated.
256 devices in a mesh: ctx: 8 (over x, z_lo), tp: 32 (over z_hi, y, core).
Axes of the slice: x: 4, y: 4, z: 8 (z_hi: 4, z_lo: 2; z = z_hi * 2 + z_lo), core: 2. Of those that a mesh axis runs over, the one named last changes fastest.
Arguments:
- states: bfloat16 [8192, 2048], P(('ctx', 'tp')), may hold values from -6 to 6
- short_lengths: int32 [64], P('ctx'), may hold values from 1 to 64, 3072 in all
- attn_gain: float32 [2048], replicated, may hold values from 0.5 to 16
- wq: bfloat16 [2048, 2048], P(None, 'tp'), may hold values from -0.125 to 0.125
- wkv: bfloat16 [2048, 512], replicated, may hold values from -0.125 to 0.125
- wo: bfloat16 [2048, 2048], P('tp'), may hold values from -0.125 to 0.125
- mlp_gain: float32 [2048], replicated, may hold values from 0.5 to 1.5
- w_gate: bfloat16 [2048, 5632], P(None, 'tp'), may hold values from -0.125 to 0.125
- w_up: bfloat16 [2048, 5632], P(None, 'tp'), may hold values from -0.125 to 0.125
- w_down: bfloat16 [5632, 2048], P('tp'), may hold values from -0.078125 to 0.078125
Outputs:
- updated: bfloat16 [8192, 2048], P(('ctx', 'tp'))
- long_cache: bfloat16 [2, 2048, 512], P(None, 'ctx', 'tp')
- short_cache: bfloat16 [64, 64, 512], P('ctx', None, 'tp')
Inputs may be any that keep to these rules, and one draw needn't show every extreme that they name: `short_lengths`: rows of a short prompt at or beyond its length are padding; the largest length is 64.
All inputs are finite; a program needn't handle non-finite values. No bound on the sum of `short_lengths` on one device may be relied on, other than what follows from the above.
Results may differ from a plain program's by a relative error of at most 0.022.
The roundings to bfloat16 on the way count: a program that leaves them out, or rounds other values in their place, can miss the bound.
Values may be sent and summed in bfloat16 or wider, within the bound.
No kernel may reach another device: no remote copies, remote signals or barrier semaphores. Data moves between devices by JAX's collectives and lax.ppermute only.
A program may use at most 64 MiB of HBM per device.

v0:
```python
import jax
import jax.numpy as jnp
from jax import lax
from jax.sharding import PartitionSpec as P

KVH = 4
HEAD_SIZE = 64
LONG = 2
LLEN = 2048
SLEN = 64
EPS = 1e-05
THETA = 10000.0
NEG = -1e30


def rms_scale(matrix, gain):
    entries = matrix.astype(jnp.float32)
    power = jnp.mean(entries * entries, axis=-1, keepdims=True)
    return (entries * lax.rsqrt(power + EPS) * gain).astype(jnp.bfloat16)


def rotate(entries, positions):
    half_width = entries.shape[-1] // 2
    frequency = THETA ** (-jnp.arange(half_width, dtype=jnp.float32) * 2.0 / entries.shape[-1])
    angles = positions.astype(jnp.float32)[:, None] * frequency[None, :]
    cosine = jnp.cos(angles)[:, None, :]
    sine_wave = jnp.sin(angles)[:, None, :]
    first_half = entries[..., :half_width]
    second_half = entries[..., half_width:]
    return jnp.concatenate(
        [
            first_half * cosine - second_half * sine_wave,
            second_half * cosine + first_half * sine_wave,
        ],
        axis=-1,
    )


def rank_positions(ctx_rank, rank_rows, block_len, long_rows, n_blocks):
    index_row = jnp.arange(rank_rows, dtype=jnp.int32)
    half_index = index_row // block_len % 2
    offset_row = index_row % block_len
    which_block = jnp.where(half_index == 0, ctx_rank, n_blocks - 1 - ctx_rank)
    long_pos = which_block * block_len + offset_row
    short_pos = (index_row - long_rows) % SLEN
    return jnp.where(index_row < long_rows, long_pos, short_pos)


def project(matrix, positions, wq, wkv_head, heads_dev):
    row_count = matrix.shape[0]
    query_matrix = jnp.dot(matrix, wq, preferred_element_type=jnp.float32).reshape(
        row_count, heads_dev, HEAD_SIZE
    )
    query_matrix = rotate(query_matrix, positions).astype(jnp.bfloat16)
    pairs = jnp.dot(matrix, wkv_head, preferred_element_type=jnp.float32)
    key_matrix = rotate(pairs[:, None, :HEAD_SIZE], positions).astype(jnp.bfloat16)[:, 0]
    value_matrix = pairs[:, HEAD_SIZE:].astype(jnp.bfloat16)
    return jnp.concatenate(
        [query_matrix.reshape(row_count, heads_dev * HEAD_SIZE), key_matrix, value_matrix], axis=1
    )


def attend(soft_state, query_matrix, query_pos, key_matrix, value_matrix, key_pos, valid_keys):
    best_score, weight_sum, weighted = soft_state
    logit_scores = jnp.einsum(
        "rzsm,rvm->rzsv", query_matrix, key_matrix, preferred_element_type=jnp.float32
    ) * HEAD_SIZE ** (-0.5)
    allowed = (key_pos[None, :] <= query_pos[:, None])[None, None] & valid_keys[:, None, None, :]
    logit_scores = jnp.where(allowed, logit_scores, NEG)
    new_best = jnp.maximum(best_score, jnp.max(logit_scores, axis=-1))
    weights = jnp.where(allowed, jnp.exp(logit_scores - new_best[..., None]), 0.0)
    weight_sum = jnp.sum(weights, axis=-1)
    weighted = jnp.einsum(
        "awlp,ape->awle",
        weights.astype(jnp.bfloat16),
        value_matrix,
        preferred_element_type=jnp.float32,
    )
    return (new_best, weight_sum, weighted)


def per_device(states, short_lengths, attn_gain, wq, wkv, wo, mlp_gain, w_gate, w_up, w_down):
    n_ctx = lax.axis_size("ctx")
    n_tp = lax.axis_size("tp")
    ctx_rank = lax.axis_index("ctx")
    tp_index = lax.axis_index("tp")
    tok_rows = states.shape[0]
    rank_rows = tok_rows * n_tp
    n_blocks = 2 * n_ctx
    block_len = LLEN // n_blocks
    long_rows = LONG * 2 * block_len
    heads_dev = wq.shape[1] // HEAD_SIZE
    q_cols = heads_dev * HEAD_SIZE
    pair_width = 2 * HEAD_SIZE
    cache_cols = KVH * pair_width // n_tp
    kv_group = tp_index * KVH // n_tp
    wkv_head = lax.dynamic_slice_in_dim(wkv, kv_group * pair_width, pair_width, 1)
    first_col = tp_index * cache_cols - kv_group * pair_width
    positions = rank_positions(ctx_rank, rank_rows, block_len, long_rows, n_blocks)
    packed = project(
        lax.all_gather(rms_scale(states, attn_gain), "tp", axis=0, tiled=True),
        positions,
        wq,
        wkv_head,
        heads_dev,
    )
    query_matrix = packed[:, :q_cols].reshape(rank_rows, heads_dev, HEAD_SIZE)
    key_matrix = packed[:, q_cols : q_cols + HEAD_SIZE]
    value_matrix = packed[:, q_cols + HEAD_SIZE :]
    long_q = (
        query_matrix[:long_rows]
        .reshape(LONG, 2 * block_len, heads_dev, HEAD_SIZE)
        .transpose(0, 2, 1, 3)
    )
    long_k = key_matrix[:long_rows].reshape(LONG, 2, 1, block_len, HEAD_SIZE)
    long_v = value_matrix[:long_rows].reshape(LONG, 2, 1, block_len, HEAD_SIZE)
    long_qpos = positions[: 2 * block_len]
    half_pick = jnp.arange(2, dtype=jnp.int32)[:, None, None]
    long_init = (
        jnp.full((LONG, heads_dev, 2 * block_len), NEG, jnp.float32),
        jnp.zeros((LONG, heads_dev, 2 * block_len), jnp.float32),
        jnp.zeros((LONG, heads_dev, 2 * block_len, HEAD_SIZE), jnp.float32),
        jnp.zeros((LONG, 2, block_len, cache_cols), jnp.float32),
    )
    gathered = lax.all_gather(jnp.stack([long_k[:, :, 0], long_v[:, :, 0]]), "ctx", axis=0)
    piece_k = jnp.moveaxis(gathered[:, 0], 0, 2)
    piece_v = jnp.moveaxis(gathered[:, 1], 0, 2)
    piece_blocks = piece_k.shape[2]
    block_ids = jnp.arange(piece_blocks, dtype=jnp.int32)
    held_blocks = jnp.stack([block_ids, n_blocks - 1 - block_ids])
    key_pos = (
        held_blocks[:, :, None] * block_len + jnp.arange(block_len, dtype=jnp.int32)
    ).reshape(-1)
    key_count = 2 * piece_blocks * block_len
    flat_k = piece_k.reshape(LONG, key_count, HEAD_SIZE)
    flat_v = piece_v.reshape(LONG, key_count, HEAD_SIZE)
    all_valid = jnp.ones((LONG, key_count), dtype=bool)
    soft_state = long_init[:3]
    soft_state = attend(soft_state, long_q, long_qpos, flat_k, flat_v, key_pos, all_valid)
    joined = jnp.concatenate([piece_k, piece_v], axis=-1)
    own_cols = lax.dynamic_slice_in_dim(joined, first_col, cache_cols, 4)
    selector = ((held_blocks[None] // 2 == ctx_rank) & (held_blocks[None] % 2 == half_pick)).astype(
        jnp.bfloat16
    )
    cache_rows = jnp.einsum(
        "ehj,phjbc->pebc", selector, own_cols, preferred_element_type=jnp.float32
    )
    folded = soft_state + (cache_rows,)
    long_out = (
        (folded[2] / folded[1][..., None])
        .astype(jnp.bfloat16)
        .transpose(0, 2, 1, 3)
        .reshape(long_rows, q_cols)
    )
    long_cache = folded[3].astype(jnp.bfloat16).reshape(LONG, 2 * block_len, cache_cols)
    short_count = short_lengths.shape[0]
    short_q = (
        query_matrix[long_rows:]
        .reshape(short_count, SLEN, heads_dev, HEAD_SIZE)
        .transpose(0, 2, 1, 3)
    )
    short_k = key_matrix[long_rows:].reshape(short_count, SLEN, HEAD_SIZE)
    short_v = value_matrix[long_rows:].reshape(short_count, SLEN, HEAD_SIZE)
    offsets = jnp.arange(SLEN, dtype=jnp.int32)
    short_valid = offsets[None, :] < short_lengths[:, None]
    short_init = (
        jnp.full((short_count, heads_dev, SLEN), NEG, jnp.float32),
        jnp.zeros((short_count, heads_dev, SLEN), jnp.float32),
        jnp.zeros((short_count, heads_dev, SLEN, HEAD_SIZE), jnp.float32),
    )
    short_state = attend(short_init, short_q, offsets, short_k, short_v, offsets, short_valid)
    short_out = (
        (short_state[2] / short_state[1][..., None])
        .astype(jnp.bfloat16)
        .transpose(0, 2, 1, 3)
        .reshape(short_count * SLEN, q_cols)
    )
    short_cache = lax.dynamic_slice_in_dim(
        jnp.concatenate([short_k, short_v], axis=-1), first_col, cache_cols, 2
    )
    attn = jnp.concatenate([long_out, short_out], axis=0)
    mixed = lax.psum_scatter(
        jnp.dot(attn, wo, preferred_element_type=jnp.float32).astype(jnp.bfloat16),
        "tp",
        scatter_dimension=0,
        tiled=True,
    ).astype(jnp.float32)
    residual = (states.astype(jnp.float32) + mixed).astype(jnp.bfloat16)
    piece = lax.all_gather(rms_scale(residual, mlp_gain), "tp", axis=0, tiled=True)
    gate = jnp.dot(piece, w_gate, preferred_element_type=jnp.float32)
    up_part = jnp.dot(piece, w_up, preferred_element_type=jnp.float32)
    hidden = (jax.nn.silu(gate) * up_part).astype(jnp.bfloat16)
    down = lax.psum_scatter(
        jnp.dot(hidden, w_down, preferred_element_type=jnp.float32).astype(jnp.bfloat16),
        "tp",
        scatter_dimension=0,
        tiled=True,
    ).astype(jnp.float32)
    updated = (residual.astype(jnp.float32) + down).astype(jnp.bfloat16)
    return (updated, long_cache, short_cache)


def solution(mesh):
    in_specs = (
        P(("ctx", "tp"), None),
        P("ctx"),
        P(),
        P(None, "tp"),
        P(),
        P("tp", None),
        P(),
        P(None, "tp"),
        P(None, "tp"),
        P("tp", None),
    )
    out_specs = (P(("ctx", "tp"), None), P(None, "ctx", "tp"), P("ctx", None, "tp"))
    return jax.shard_map(
        per_device, mesh=mesh, in_specs=in_specs, out_specs=out_specs, check_vma=False
    )
```

profile of v0, /device:TPU:2, one launch (start us, length us, event | category | flops | bytes accessed | tf_op | source)
XLA Modules:
  0.0 415.9 jit_solution(9527063426652451580)
XLA Ops:
  7.2 1.2 fusion.28
  8.4 1.7 fusion.30
  10.3 64.2 %all-gather.5.cloned.1.call-done = bf16[1024,2048]{1,0:T(8,128)(2,1)} async-done(((bf16[32,2048]{1,0:T(8,128)(2,1)}), bf16[1024,2048]{1,0:T(8,128)(2,1)}) %all-gather.5.cloned.1.call-update) | async-done | bytes 4194320 | tf_op jit(solution)/shard_map/all_gather | solution.py:101
  74.5 3.7 fusion.106
  78.3 3.6 convolution_bitcast_fusion
  83.9 1.2 broadcast_compare_fusion
  86.5 36.2 %all-gather.9.cloned.1.call-done = bf16[16,2,2,128,64]{3,4,2,1,0:T(8,128)(2,1)} async-done(((bf16[2,2,2,128,64]{3,4,2,1,0:T(8,128)(2,1)}), bf16[16,2,2,128,64]{3,4,2,1,0:T(8,128)(2,1)}) %all-gather.9.cloned.1.call-update) | async-done | bytes 1048592 | tf_op jit(solution)/shard_map/all_gather | solution.py:125
  122.7 2.1 fusion.103
  125.2 1.0 reshape.506
  126.2 1.4 copy.65
  127.6 1.0 reshape.507
  128.6 2.4 fusion
  131.0 1.4 fusion.1
  132.4 1.1 fusion.17
  133.6 3.2 convolution_convert_fusion.1
  136.9 100.0 %reduce-scatter.3.cloned.1.call-done = bf16[32,2048]{1,0:T(8,128)(2,1)} async-done(((bf16[1024,2048]{1,0:T(8,128)(2,1)}), bf16[32,2048]{1,0:T(8,128)(2,1)}) %reduce-scatter.3.cloned.1.call-update) | async-done | bytes 131088 | tf_op jit(solution)/shard_map/reduce_scatter | solution.py:182
  236.9 1.1 fusion.32
  238.0 1.7 fusion.34
  239.9 57.9 %all-gather.7.cloned.1.call-done = bf16[1024,2048]{1,0:T(8,128)(2,1)} async-done(((bf16[32,2048]{1,0:T(8,128)(2,1)}), bf16[1024,2048]{1,0:T(8,128)(2,1)}) %all-gather.7.cloned.1.call-update) | async-done | bytes 4194320 | tf_op jit(solution)/shard_map/all_gather | solution.py:189
  297.9 4.8 %fusion.107 = f32[1024,176]{0,1:T(8,128)} fusion(bf16[1024,2048]{1,0:T(8,128)(2,1)} %all-gather.7.cloned.1.call-done, bf16[2048,176]{0,1:T(8,128)(2,1)} %param.17), kind=kOutput, calls=%fused_computation.160 | convolution fusion | flops 738197504 | bytes 5636096 | tf_op jit(solution)/shard_map/dot_general | solution.py:190
  302.7 7.5 %convolution_convert_fusion = bf16[1024,2048]{1,0:T(8,128)(2,1)} fusion(bf16[176,2048]{1,0:T(8,128)(2,1)} %param.19, bf16[1024,2048]{1,0:T(8,128)(2,1)} %all-gather.7.cloned.1.call-done, bf16[2048,176]{0,1:T(8,128)(2,1)} %param.18, f32[1024,176]{0,1:T(8,128)} %fusion.107), kind=kOutput, calls=%fused_computation.2 | convolution fusion | flops 1479573504 | bytes 10551296 | tf_op jit(solution)/shard_map/dot_general | solution.py:194
  310.9 0.9 copy.44
  313.3 94.4 %reduce-scatter.5.cloned.1.call-done = bf16[32,2048]{1,0:T(8,128)(2,1)} async-done(((bf16[1024,2048]{1,0:T(8,128)(2,1)}), bf16[32,2048]{1,0:T(8,128)(2,1)}) %reduce-scatter.5.cloned.1.call-update) | async-done | bytes 131088 | tf_op jit(solution)/shard_map/reduce_scatter | solution.py:193
  407.8 1.6 fusion.35
  (75 shorter events, 6.5 us)
Async XLA Ops:
  7.2 67.3 %copy-start = (bf16[2048,512]{1,0:T(8,128)(2,1)S(1)}, bf16[2048,512]{1,0:T(8,128)(2,1)}, u32[]{:S(2)}) copy-start(bf16[2048,512]{1,0:T(8,128)(2,1)} %param.14) | copy-start | bytes 6291460
  7.2 67.3 %all-gather.5.cloned.1.call-start = ((), (), s32[]{:S(2)}) async-start(), calls=%async_computation.2 | async-start | bytes 4325376 | tf_op jit(solution)/shard_map/all_gather | solution.py:101
  10.1 112.6 %all-gather.9.cloned.1.call-start = ((), (), s32[]{:S(2)}) async-start(), calls=%async_computation.6 | async-start | bytes 1179648 | tf_op jit(solution)/shard_map/all_gather | solution.py:125
  10.2 68.0 %copy-start.9 = (s32[1024]{0:T(1024)}, s32[1024]{0:T(1024)S(1)}, u32[]{:S(2)}) copy-start(s32[1024]{0:T(1024)S(1)} %fusion.78) | copy-start | bytes 12292
  10.3 68.0 %copy-start.6 = (bf16[2048,64]{0,1:T(8,128)(2,1)S(1)}, bf16[2048,64]{0,1:T(8,128)(2,1)}, u32[]{:S(2)}) copy-start(bf16[2048,64]{0,1:T(8,128)(2,1)} %param.13) | copy-start | bytes 786436
  78.2 5.1 %copy-start.12 = (s32[8]{0:T(128)S(1)}, s32[8]{0:T(128)}, u32[]{:S(2)}) copy-start(s32[8]{0:T(128)} %param.11) | copy-start | bytes 100
  78.2 5.7 %slice-start = ((s32[1024]{0:T(1024)}), s32[256]{0:T(256)S(1)}, s32[]{:S(2)}) async-start(s32[1024]{0:T(1024)} %copy-done.9), calls=%async_computation.7 | async-start | bytes 2048 | tf_op jit(solution)/shard_map/slice | solution.py:117
  83.3 153.7 %reduce-scatter.3.cloned.1.call-start = ((), (), s32[]{:S(2)}) async-start(), calls=%async_computation.3 | async-start | bytes 4325376 | tf_op jit(solution)/shard_map/reduce_scatter | solution.py:182
  83.3 0.5 copy-start.10
  85.4 39.4 %copy-start.5 = (bf16[8,64,64]{1,0,2:T(8,128)(2,1)}, bf16[8,64,64]{1,0,2:T(8,128)(2,1)S(1)}, u32[]{:S(2)}) copy-start(bf16[8,64,64]{1,0,2:T(8,128)(2,1)S(1)} %reshape.509) | copy-start | bytes 196612
  128.6 2.4 copy-start.1
  128.6 3.8 copy-start.4
  132.4 1.2 copy-start.7
  133.6 103.4 %copy-start.2 = (bf16[32,2048]{1,0:T(8,128)(2,1)S(1)}, bf16[32,2048]{1,0:T(8,128)(2,1)}, u32[]{:S(2)}) copy-start(bf16[32,2048]{1,0:T(8,128)(2,1)} %param.10) | copy-start | bytes 393220
  133.6 104.4 %copy-start.8 = (f32[2048]{0:T(1024)S(1)}, f32[2048]{0:T(1024)}, u32[]{:S(2)}) copy-start(f32[2048]{0:T(1024)} %param.16) | copy-start | bytes 24580
  136.9 161.0 %all-gather.7.cloned.1.call-start = ((), (), s32[]{:S(2)}) async-start(), calls=%async_computation.4 | async-start | bytes 4325376 | tf_op jit(solution)/shard_map/all_gather | solution.py:189
  239.7 168.1 %reduce-scatter.5.cloned.1.call-start = ((), (), s32[]{:S(2)}) async-start(), calls=%async_computation.5 | async-start | bytes 4325376 | tf_op jit(solution)/shard_map/reduce_scatter | solution.py:193
  310.2 0.7 copy-start.11
  310.2 97.6 %copy-start.3 = (bf16[32,2048]{1,0:T(8,128)(2,1)S(1)}, bf16[32,2048]{1,0:T(8,128)(2,1)}, u32[]{:S(2)}) copy-start(bf16[32,2048]{1,0:T(8,128)(2,1)} %reduce-scatter.3.cloned.1.call-done) | copy-start | bytes 393220
Sparse Core Ops, SparseCore 0:
  11.1 63.2 all-gather.4
  83.4 39.3 all-gather.8
  137.0 99.9 reduce-scatter.2
  240.2 57.5 all-gather.6
  310.3 97.3 reduce-scatter.4
where the time goes:
time: 416 us
  waiting for transfers between devices  353 us (85%)
  matrix products  27.3 us (7%)
  between operations  14.1 us (3%)
  other arithmetic  12.1 us (3%)
  local copies, waits for them, and re-layouts  9.11 us (2%)
    reduce_scatter x1, waiting for transfers between devices, per_device(): lax.psum_scatter(jnp.dot(attn, wo, preferred_element_type=jnp.float32).as...  100 us
    reduce_scatter x1, waiting for transfers between devices, per_device(): lax.psum_scatter(jnp.dot(hidden, w_down, preferred_element_type=jnp.float...  94.4 us
    all_gather x1, waiting for transfers between devices, per_device(): lax.all_gather(rms_scale(states, attn_gain), 'tp', axis=0, tiled=True)  64.2 us
    all_gather x1, waiting for transfers between devices, per_device(): lax.all_gather(rms_scale(residual, mlp_gain), 'tp', axis=0, tiled=True)  57.9 us
    all_gather x1, waiting for transfers between devices, per_device(): lax.all_gather(jnp.stack([long_k[:, :, 0], long_v[:, :, 0]]), 'ctx', axis=0)  36.2 us
  transfers between devices with their start and end apart: 5, of which 5 were waited for; matrix products, arithmetic and copies ran while one was open for 1% of the time, Pallas kernels for 0%

commit v1 on v0

--- a/solution.py
+++ b/solution.py
@@ -186,7 +186,12 @@
         tiled=True,
     ).astype(jnp.float32)
     residual = (states.astype(jnp.float32) + mixed).astype(jnp.bfloat16)
-    piece = lax.all_gather(rms_scale(residual, mlp_gain), "tp", axis=0, tiled=True)
+    piece = jnp.concatenate(
+        lax.all_to_all(
+            jnp.stack([rms_scale(residual, mlp_gain)] * lax.axis_size("tp")), "tp", 0, 0
+        ),
+        axis=0,
+    )
     gate = jnp.dot(piece, w_gate, preferred_element_type=jnp.float32)
     up_part = jnp.dot(piece, w_up, preferred_element_type=jnp.float32)
     hidden = (jax.nn.silu(gate) * up_part).astype(jnp.bfloat16)

time: 416 us -> 459 us (1.10)
  blocking collectives: 0 us -> 101 us
  waiting for transfers between devices: 353 us -> 295 us
    all_to_all x0 -> x1, blocking collectives: none -> 101 us  [per_device(): lax.all_to_all(jnp.stack([rms_scale(residual, mlp_gain)] * lax.axis_size(...]
    all_gather x1 -> x0, waiting for transfers between devices: 57.9 us -> none  [per_device(): lax.all_gather(rms_scale(residual, mlp_gain), 'tp', axis=0, tiled=True)]
  transfers between devices with their start and end apart: 5 -> 4, of which waited for: 5 -> 4; matrix products, arithmetic and copies ran while one was open for 1% -> 1% of each run, Pallas kernels for 0% -> 0%
where the time goes in v1:
time: 459 us
  waiting for transfers between devices  295 us (64%)
  blocking collectives  101 us (22%)
  matrix products  24.9 us (5%)
  between operations  14.2 us (3%)
  local copies, waits for them, and re-layouts  11.6 us (3%)
  other arithmetic  11.4 us (2%)
    all_to_all x1, blocking collectives, per_device(): lax.all_to_all(jnp.stack([rms_scale(residual, mlp_gain)] * lax.axis_size(...  101 us
    reduce_scatter x1, waiting for transfers between devices, per_device(): lax.psum_scatter(jnp.dot(attn, wo, preferred_element_type=jnp.float32).as...  100 us
    reduce_scatter x1, waiting for transfers between devices, per_device(): lax.psum_scatter(jnp.dot(hidden, w_down, preferred_element_type=jnp.float...  94.8 us
    all_gather x1, waiting for transfers between devices, per_device(): lax.all_gather(rms_scale(states, attn_gain), 'tp', axis=0, tiled=True)  64.2 us
    all_gather x1, waiting for transfers between devices, per_device(): lax.all_gather(jnp.stack([long_k[:, :, 0], long_v[:, :, 0]]), 'ctx', axis=0)  36.2 us
  transfers between devices with their start and end apart: 4, of which 4 were waited for; matrix products, arithmetic and copies ran while one was open for 1% of the time, Pallas kernels for 0%

profile of v1, /device:TPU:2, one launch (start us, length us, event | category | flops | bytes accessed | tf_op | source)
XLA Modules:
  0.0 458.7 jit_solution(1070852615516728946)
XLA Ops:
  7.2 1.2 fusion.28
  8.4 1.7 fusion.30
  10.3 64.2 %all-gather.4.cloned.1.call-done = bf16[1024,2048]{1,0:T(8,128)(2,1)} async-done(((bf16[32,2048]{1,0:T(8,128)(2,1)}), bf16[1024,2048]{1,0:T(8,128)(2,1)}) %all-gather.4.cloned.1.call-update) | async-done | bytes 4194320 | tf_op jit(solution)/shard_map/all_gather | solution.py:101
  74.5 3.7 fusion.106
  78.3 3.6 convolution_bitcast_fusion
  83.9 1.2 broadcast_compare_fusion
  86.5 36.2 %all-gather.6.cloned.1.call-done = bf16[16,2,2,128,64]{3,4,2,1,0:T(8,128)(2,1)} async-done(((bf16[2,2,2,128,64]{3,4,2,1,0:T(8,128)(2,1)}), bf16[16,2,2,128,64]{3,4,2,1,0:T(8,128)(2,1)}) %all-gather.6.cloned.1.call-update) | async-done | bytes 1048592 | tf_op jit(solution)/shard_map/all_gather | solution.py:125
  122.7 2.1 fusion.103
  125.2 1.0 reshape.511
  126.2 1.4 copy.65
  127.6 1.0 reshape.512
  128.6 2.4 fusion
  131.0 1.4 fusion.1
  132.4 1.1 fusion.17
  133.6 3.2 convolution_convert_fusion.1
  136.9 100.1 %reduce-scatter.3.cloned.1.call-done = bf16[32,2048]{1,0:T(8,128)(2,1)} async-done(((bf16[1024,2048]{1,0:T(8,128)(2,1)}), bf16[32,2048]{1,0:T(8,128)(2,1)}) %reduce-scatter.3.cloned.1.call-update) | async-done | bytes 131088 | tf_op jit(solution)/shard_map/reduce_scatter | solution.py:182
  237.0 1.1 fusion.32
  238.1 1.0 fusion.34
  239.6 101.1 %all_to_all.5 = bf16[32,32,2048]{2,1,0:T(8,128)(2,1)S(1)} all-to-all(bf16[32,32,2048]{2,1,0:T(8,128)(2,1)S(1)} %stack.8), channel_id=1, replica_groups=mesh['ctx'=8,'tp'=32] {'tp'}, dimensions={0} | all-to-all | bytes 8388608 | tf_op jit(solution)/shard_map/all_to_all | solution.py:190
  340.7 2.0 copy-done.2
  342.7 2.5 fusion.107
  345.2 7.5 %convolution_convert_fusion = bf16[1024,2048]{1,0:T(8,128)(2,1)} fusion(bf16[176,2048]{1,0:T(8,128)(2,1)} %param.19, bf16[1024,2048]{1,0:T(8,128)(2,1)} %bitcast.74, bf16[2048,176]{0,1:T(8,128)(2,1)} %param.18, f32[1024,176]{0,1:T(8,128)} %fusion.107), kind=kOutput, calls=%fused_computation.2 | convolution fusion | flops 1479573504 | bytes 10551296 | tf_op jit(solution)/shard_map/dot_general | solution.py:199
  355.8 94.8 %reduce-scatter.5.cloned.1.call-done = bf16[32,2048]{1,0:T(8,128)(2,1)} async-done(((bf16[1024,2048]{1,0:T(8,128)(2,1)}), bf16[32,2048]{1,0:T(8,128)(2,1)}) %reduce-scatter.5.cloned.1.call-update) | async-done | bytes 131088 | tf_op jit(solution)/shard_map/reduce_scatter | solution.py:198
  450.6 1.6 fusion.35
  (78 shorter events, 7.7 us)
Async XLA Ops:
  7.2 67.3 %copy-start = (bf16[2048,512]{1,0:T(8,128)(2,1)S(1)}, bf16[2048,512]{1,0:T(8,128)(2,1)}, u32[]{:S(2)}) copy-start(bf16[2048,512]{1,0:T(8,128)(2,1)} %param.14) | copy-start | bytes 6291460
  7.2 67.3 %all-gather.4.cloned.1.call-start = ((), (), s32[]{:S(2)}) async-start(), calls=%async_computation.3 | async-start | bytes 4325376 | tf_op jit(solution)/shard_map/all_gather | solution.py:101
  10.1 112.6 %all-gather.6.cloned.1.call-start = ((), (), s32[]{:S(2)}) async-start(), calls=%async_computation.6 | async-start | bytes 1179648 | tf_op jit(solution)/shard_map/all_gather | solution.py:125
  10.2 68.0 %copy-start.10 = (s32[1024]{0:T(1024)}, s32[1024]{0:T(1024)S(1)}, u32[]{:S(2)}) copy-start(s32[1024]{0:T(1024)S(1)} %fusion.78) | copy-start | bytes 12292
  10.3 68.0 %copy-start.7 = (bf16[2048,64]{0,1:T(8,128)(2,1)S(1)}, bf16[2048,64]{0,1:T(8,128)(2,1)}, u32[]{:S(2)}) copy-start(bf16[2048,64]{0,1:T(8,128)(2,1)} %param.13) | copy-start | bytes 786436
  78.2 5.1 %copy-start.14 = (s32[8]{0:T(128)S(1)}, s32[8]{0:T(128)}, u32[]{:S(2)}) copy-start(s32[8]{0:T(128)} %param.11) | copy-start | bytes 100
  78.2 5.7 %slice-start = ((s32[1024]{0:T(1024)}), s32[256]{0:T(256)S(1)}, s32[]{:S(2)}) async-start(s32[1024]{0:T(1024)} %copy-done.10), calls=%async_computation.7 | async-start | bytes 2048 | tf_op jit(solution)/shard_map/slice | solution.py:117
  83.3 153.8 %reduce-scatter.3.cloned.1.call-start = ((), (), s32[]{:S(2)}) async-start(), calls=%async_computation.4 | async-start | bytes 4325376 | tf_op jit(solution)/shard_map/reduce_scatter | solution.py:182
  83.3 0.5 copy-start.11
  85.4 39.5 %copy-start.6 = (bf16[8,64,64]{1,0,2:T(8,128)(2,1)}, bf16[8,64,64]{1,0,2:T(8,128)(2,1)S(1)}, u32[]{:S(2)}) copy-start(bf16[8,64,64]{1,0,2:T(8,128)(2,1)S(1)} %reshape.514) | copy-start | bytes 196612
  128.6 2.4 copy-start.1
  128.6 3.8 copy-start.5
  132.4 1.2 copy-start.8
  133.6 103.4 %copy-start.3 = (bf16[32,2048]{1,0:T(8,128)(2,1)S(1)}, bf16[32,2048]{1,0:T(8,128)(2,1)}, u32[]{:S(2)}) copy-start(bf16[32,2048]{1,0:T(8,128)(2,1)} %param.10) | copy-start | bytes 393220
  133.6 104.5 %copy-start.9 = (f32[2048]{0:T(1024)S(1)}, f32[2048]{0:T(1024)}, u32[]{:S(2)}) copy-start(f32[2048]{0:T(1024)} %param.16) | copy-start | bytes 24580
  136.9 313.7 %reduce-scatter.5.cloned.1.call-start = ((), (), s32[]{:S(2)}) async-start(), calls=%async_computation.5 | async-start | bytes 4325376 | tf_op jit(solution)/shard_map/reduce_scatter | solution.py:198
  239.6 103.1 %copy-start.13 = (bf16[2048,176]{0,1:T(8,128)(2,1)S(1)}, bf16[2048,176]{0,1:T(8,128)(2,1)}, u32[]{:S(2)}) copy-start(bf16[2048,176]{0,1:T(8,128)(2,1)} %param.17) | copy-start | bytes 2162692
  340.7 2.0 copy-start.2
  352.6 0.7 copy-start.12
  352.6 97.9 %copy-start.4 = (bf16[32,2048]{1,0:T(8,128)(2,1)S(1)}, bf16[32,2048]{1,0:T(8,128)(2,1)}, u32[]{:S(2)}) copy-start(bf16[32,2048]{1,0:T(8,128)(2,1)} %reduce-scatter.3.cloned.1.call-done) | copy-start | bytes 393220
Sparse Core Ops, SparseCore 0:
  11.1 63.2 all-gather.3
  83.4 39.3 all-gather.5
  137.0 99.9 reduce-scatter.2
  352.8 97.7 reduce-scatter.4
